TPU v7x, 32 devices: a whole 2x2x4 slice. The times are simulated.
32 devices in a mesh: dp: 4 (over x, core), seq: 8 (over z, y).
Axes of the slice: x: 2, y: 2, z: 4, core: 2. Of those that a mesh axis runs over, the one named last changes fastest.
Arguments:
- inputs: bfloat16 [2, 4, 1024, 768], P(None, 'dp', 'seq'), may hold values from -6 to 6
- cotangent: bfloat16 [2, 4, 1024, 768], P(None, 'dp', 'seq'), may hold values from -6 to 6
- bounds: int32 [2, 4, 2, 2], P(None, 'dp'), may hold values from 0 to 1024, as said below
- ln1_gain: bfloat16 [768], P(('dp', 'seq')), may hold values from 0.5 to 1.5
- ln1_bias: bfloat16 [768], P(('dp', 'seq')), may hold values from -1 to 1
- w_qkv: bfloat16 [768, 2304], P(('dp', 'seq')), may hold values from -0.21875 to 0.21875
- b_query: bfloat16 [768], P(('dp', 'seq')), may hold values from -1.5 to 1.5
- b_value: bfloat16 [768], P(('dp', 'seq')), may hold values from -1.5 to 1.5
- w_out: bfloat16 [768, 768], P(('dp', 'seq')), may hold values from -1.25 to 1.25
- b_out: bfloat16 [768], P(('dp', 'seq')), may hold values from -1.5 to 1.5
- ln2_gain: bfloat16 [768], P(('dp', 'seq')), may hold values from 0.5 to 1.5
- ln2_bias: bfloat16 [768], P(('dp', 'seq')), may hold values from -1 to 1
- w_up: bfloat16 [768, 3072], P(('dp', 'seq')), may hold values from -0.21875 to 0.21875
- b_up: bfloat16 [3072], P(('dp', 'seq')), may hold values from -1.5 to 1.5
- w_down: bfloat16 [3072, 768], P(('dp', 'seq')), may hold values from -0.109375 to 0.109375
- b_down: bfloat16 [768], P(('dp', 'seq')), may hold values from -1.5 to 1.5
Outputs:
- outputs: bfloat16 [2, 4, 1024, 768], P(None, 'dp', 'seq')
- input_grad: bfloat16 [2, 4, 1024, 768], P(None, 'dp', 'seq')
- grad_ln1_gain: float32 [768], P(('dp', 'seq'))
- grad_ln1_bias: float32 [768], P(('dp', 'seq'))
- grad_w_qkv: float32 [768, 2304], P(('dp', 'seq'))
- grad_b_query: float32 [768], P(('dp', 'seq'))
- grad_b_value: float32 [768], P(('dp', 'seq'))
- grad_w_out: float32 [768, 768], P(('dp', 'seq'))
- grad_b_out: float32 [768], P(('dp', 'seq'))
- grad_ln2_gain: float32 [768], P(('dp', 'seq'))
- grad_ln2_bias: float32 [768], P(('dp', 'seq'))
- grad_w_up: float32 [768, 3072], P(('dp', 'seq'))
- grad_b_up: float32 [3072], P(('dp', 'seq'))
- grad_w_down: float32 [3072, 768], P(('dp', 'seq'))
- grad_b_down: float32 [768], P(('dp', 'seq'))
Inputs may be any that keep to these rules, and one draw needn't show every extreme that they name: `bounds`: for each sequence, 2 picture pieces [start, end) of exactly 256 rows each, in increasing order and not intersecting.
All inputs are finite; a program needn't handle non-finite values.
Results may differ from a plain program's by a relative error of at most 0.02.
Values may be sent and summed in bfloat16 or wider, within the bound.
No kernel may reach another device: no remote copies, remote signals or barrier semaphores. Data moves between devices by JAX's collectives and lax.ppermute only.
A program may use at most 256 MiB of HBM per device.

v0:
```python
from functools import partial
import jax
import jax.numpy as jnp
from jax import lax
from jax.sharding import PartitionSpec as P

HEADS = 12
HEAD = 64
EPSILON = 1e-05


def layer_norm(values, ln_gain, ln_shift):
    center = jnp.mean(values, axis=-1, keepdims=True)
    centered = values - center
    spread = jnp.mean(centered * centered, axis=-1, keepdims=True)
    return centered * lax.rsqrt(spread + EPSILON) * ln_gain + ln_shift


def piece_label(positions, bounds):
    inside = (positions[:, None] >= bounds[None, :, 0]) & (positions[:, None] < bounds[None, :, 1])
    labels = jnp.arange(1, bounds.shape[0] + 1, dtype=jnp.int32)
    return jnp.sum(jnp.where(inside, labels[None, :], 0), axis=1) - 1


def allowed_mask(query_pos, key_pos, bounds):
    query_label = piece_label(query_pos, bounds)
    key_label = piece_label(key_pos, bounds)
    causal = key_pos[None, :] <= query_pos[:, None]
    same_piece = (query_label[:, None] == key_label[None, :]) & (query_label[:, None] >= 0)
    return causal | same_piece


def outer_rows(left, right):
    return lax.dot_general(
        left, right, (((0,), (0,)), ((), ())), preferred_element_type=jnp.float32
    )


def times_transposed(left, right):
    return lax.dot_general(
        left, right, (((1,), (1,)), ((), ())), preferred_element_type=jnp.float32
    )


def key_step():
    return 512


def masked_weights(query_heads, key_heads, query_pos, key_pos, bounds):
    factor = query_heads.shape[2] ** (-0.5)
    scores = (
        jnp.einsum("rhd,khd->hrk", query_heads, key_heads, preferred_element_type=jnp.float32)
        * factor
    )
    allowed = allowed_mask(query_pos, key_pos, bounds)
    return jnp.where(allowed[None], jnp.exp(scores), 0.0)


def forward_fold(query_heads, query_pos, bounds):
    head_count = query_heads.shape[1]

    def fold_keys(carry, piece, first_row):
        key_piece, value_piece = piece
        piece_len = key_piece.shape[0]
        step_len = key_step()

        def inner_step(block_idx, partial_sums):
            weighted, totals = partial_sums
            offset = block_idx * step_len
            key_heads = lax.dynamic_slice_in_dim(key_piece, offset, step_len, 0).reshape(
                step_len, head_count, -1
            )
            value_heads = lax.dynamic_slice_in_dim(value_piece, offset, step_len, 0).reshape(
                step_len, head_count, -1
            )
            key_pos = offset + jnp.arange(step_len, dtype=jnp.int32)
            weights = masked_weights(query_heads, key_heads, query_pos, key_pos, bounds)
            weighted = weighted + jnp.einsum(
                "hrk,khd->rhd",
                weights.astype(jnp.bfloat16),
                value_heads,
                preferred_element_type=jnp.float32,
            )
            return (weighted, totals + jnp.sum(weights, axis=-1))

        return lax.fori_loop(0, piece_len // step_len, inner_step, carry)

    return fold_keys


def backward_fold(query_heads, query_pos, bounds, grad_heads, delta):
    head_count = query_heads.shape[1]
    factor = query_heads.shape[2] ** (-0.5)

    def fold_grads(carry, piece, first_row):
        key_piece, value_piece = piece
        piece_len = key_piece.shape[0]
        step_len = key_step()

        def inner_step(block_idx, partial_sums):
            query_grad, key_grad, value_grad = partial_sums
            offset = block_idx * step_len
            key_heads = lax.dynamic_slice_in_dim(key_piece, offset, step_len, 0).reshape(
                step_len, head_count, -1
            )
            value_heads = lax.dynamic_slice_in_dim(value_piece, offset, step_len, 0).reshape(
                step_len, head_count, -1
            )
            key_pos = offset + jnp.arange(step_len, dtype=jnp.int32)
            weights = masked_weights(query_heads, key_heads, query_pos, key_pos, bounds)
            products = jnp.einsum(
                "rhd,khd->hrk", grad_heads, value_heads, preferred_element_type=jnp.float32
            )
            score_grad = (weights * (products - delta[:, :, None])).astype(jnp.bfloat16)
            query_grad = (
                query_grad
                + jnp.einsum(
                    "hrk,khd->rhd", score_grad, key_heads, preferred_element_type=jnp.float32
                )
                * factor
            )
            key_rows = (
                jnp.einsum(
                    "hrk,rhd->khd", score_grad, query_heads, preferred_element_type=jnp.float32
                )
                * factor
            ).reshape(step_len, -1)
            value_rows = jnp.einsum(
                "hrk,rhd->khd",
                weights.astype(jnp.bfloat16),
                grad_heads,
                preferred_element_type=jnp.float32,
            ).reshape(step_len, -1)
            key_grad = lax.dynamic_update_slice_in_dim(key_grad, key_rows, offset, 0)
            value_grad = lax.dynamic_update_slice_in_dim(value_grad, value_rows, offset, 0)
            return (query_grad, key_grad, value_grad)

        return lax.fori_loop(0, piece_len // step_len, inner_step, carry)

    return fold_grads


def body(
    inputs,
    cotangent,
    bounds,
    ln1_gain,
    ln1_bias,
    w_qkv,
    b_query,
    b_value,
    w_out,
    b_out,
    ln2_gain,
    ln2_bias,
    w_up,
    b_up,
    w_down,
    b_down,
):
    shards = (
        ln1_gain,
        ln1_bias,
        w_qkv,
        b_query,
        b_value,
        w_out,
        b_out,
        ln2_gain,
        ln2_bias,
        w_up,
        b_up,
        w_down,
        b_down,
    )
    micro_count = inputs.shape[0]
    row_count = inputs.shape[2]
    width = inputs.shape[3]
    total_len = row_count * lax.axis_size("seq")
    query_pos = lax.axis_index("seq") * row_count + jnp.arange(row_count, dtype=jnp.int32)
    grad_sums = [None] * 13
    outputs_list = []
    input_grads = []
    for micro_idx in range(micro_count):
        gathered = (
            lax.all_gather(shards[0], ("dp", "seq"), axis=0, tiled=True),
            lax.all_gather(shards[1], ("dp", "seq"), axis=0, tiled=True),
            lax.all_gather(shards[2], ("dp", "seq"), axis=0, tiled=True),
            lax.all_gather(shards[3], ("dp", "seq"), axis=0, tiled=True),
            lax.all_gather(shards[4], ("dp", "seq"), axis=0, tiled=True),
            lax.all_gather(shards[5], ("dp", "seq"), axis=0, tiled=True),
            lax.all_gather(shards[6], ("dp", "seq"), axis=0, tiled=True),
            lax.all_gather(shards[7], ("dp", "seq"), axis=0, tiled=True),
            lax.all_gather(shards[8], ("dp", "seq"), axis=0, tiled=True),
            lax.all_gather(shards[9], ("dp", "seq"), axis=0, tiled=True),
            lax.all_gather(shards[10], ("dp", "seq"), axis=0, tiled=True),
            lax.all_gather(shards[11], ("dp", "seq"), axis=0, tiled=True),
            lax.all_gather(shards[12], ("dp", "seq"), axis=0, tiled=True),
        )
        (
            gain_one,
            shift_one,
            proj_qkv,
            bias_query,
            bias_value,
            proj_out,
            bias_out,
            gain_two,
            shift_two,
            proj_up,
            bias_up,
            proj_down,
            bias_down,
        ) = gathered
        seq_bounds = bounds[micro_idx, 0]
        seq_in = inputs[micro_idx, 0].astype(jnp.float32)
        normed_f, norm_one_back = jax.vjp(
            layer_norm, seq_in, gain_one.astype(jnp.float32), shift_one.astype(jnp.float32)
        )
        normed = normed_f.astype(jnp.bfloat16)
        projected = jnp.dot(normed, proj_qkv, preferred_element_type=jnp.float32)
        queries = (projected[:, :width] + bias_query.astype(jnp.float32)).astype(jnp.bfloat16)
        keys_now = projected[:, width : 2 * width].astype(jnp.bfloat16)
        values_now = (projected[:, 2 * width :] + bias_value.astype(jnp.float32)).astype(
            jnp.bfloat16
        )
        query_heads = queries.reshape(row_count, HEADS, HEAD)
        start_sums = (
            jnp.zeros((row_count, HEADS, HEAD), jnp.float32),
            jnp.zeros((HEADS, row_count), jnp.float32),
        )
        fold_keys = forward_fold(query_heads, query_pos, seq_bounds)
        weighted, totals = fold_keys(
            start_sums,
            (
                lax.all_gather(keys_now, "seq", axis=0, tiled=True),
                lax.all_gather(values_now, "seq", axis=0, tiled=True),
            ),
            jnp.int32(0),
        )
        attended = weighted / totals.T[:, :, None]
        attended_b = attended.reshape(row_count, width).astype(jnp.bfloat16)
        branch = jnp.dot(
            attended_b, proj_out, preferred_element_type=jnp.float32
        ) + bias_out.astype(jnp.float32)
        middle = seq_in + branch
        normed_two_f, norm_two_back = jax.vjp(
            layer_norm, middle, gain_two.astype(jnp.float32), shift_two.astype(jnp.float32)
        )
        normed_two = normed_two_f.astype(jnp.bfloat16)
        hidden = jnp.dot(normed_two, proj_up, preferred_element_type=jnp.float32) + bias_up.astype(
            jnp.float32
        )
        activated_f, gelu_back = jax.vjp(partial(jax.nn.gelu, approximate=False), hidden)
        activated = activated_f.astype(jnp.bfloat16)
        mlp_out = jnp.dot(
            activated, proj_down, preferred_element_type=jnp.float32
        ) + bias_down.astype(jnp.float32)
        outputs_list.append((middle + mlp_out).astype(jnp.bfloat16))
        qkv_back, out_back, up_back, down_back = (
            lax.all_gather(w_qkv, ("dp", "seq"), axis=0, tiled=True),
            lax.all_gather(w_out, ("dp", "seq"), axis=0, tiled=True),
            lax.all_gather(w_up, ("dp", "seq"), axis=0, tiled=True),
            lax.all_gather(w_down, ("dp", "seq"), axis=0, tiled=True),
        )
        out_grad = cotangent[micro_idx, 0]
        out_grad_f = out_grad.astype(jnp.float32)
        grad_down = outer_rows(activated, out_grad)
        grad_bias_down = jnp.sum(out_grad_f, axis=0)
        act_grad = times_transposed(out_grad, down_back)
        (hidden_grad,) = gelu_back(act_grad)
        hidden_grad_b = hidden_grad.astype(jnp.bfloat16)
        grad_up = outer_rows(normed_two, hidden_grad_b)
        grad_bias_up = jnp.sum(hidden_grad_b.astype(jnp.float32), axis=0)
        normed_two_grad = times_transposed(hidden_grad_b, up_back)
        middle_ln_grad, grad_gain_two, grad_shift_two = norm_two_back(normed_two_grad)
        middle_grad = out_grad_f + middle_ln_grad
        branch_grad = middle_grad.astype(jnp.bfloat16)
        grad_out = outer_rows(attended_b, branch_grad)
        grad_bias_out = jnp.sum(branch_grad.astype(jnp.float32), axis=0)
        attended_grad = times_transposed(branch_grad, out_back).astype(jnp.bfloat16)
        attended_grad_f = attended_grad.astype(jnp.float32).reshape(row_count, HEADS, HEAD)
        delta = jnp.sum(attended_grad_f * attended, axis=-1).T / totals
        grad_heads = (attended_grad_f / totals.T[:, :, None]).astype(jnp.bfloat16)
        start_grads = (
            jnp.zeros((row_count, HEADS, HEAD), jnp.float32),
            jnp.zeros((total_len, width), jnp.float32),
            jnp.zeros((total_len, width), jnp.float32),
        )
        fold_grads = backward_fold(query_heads, query_pos, seq_bounds, grad_heads, delta)
        folded = fold_grads(
            start_grads,
            (
                lax.all_gather(keys_now, "seq", axis=0, tiled=True),
                lax.all_gather(values_now, "seq", axis=0, tiled=True),
            ),
            jnp.int32(0),
        )
        query_grad = folded[0]
        key_own, value_own = (
            lax.psum_scatter(
                folded[1].astype(jnp.bfloat16), "seq", scatter_dimension=0, tiled=True
            ).astype(jnp.float32),
            lax.psum_scatter(
                folded[2].astype(jnp.bfloat16), "seq", scatter_dimension=0, tiled=True
            ).astype(jnp.float32),
        )
        query_grad_b = query_grad.reshape(row_count, width).astype(jnp.bfloat16)
        key_grad_b = key_own.astype(jnp.bfloat16)
        value_grad_b = value_own.astype(jnp.bfloat16)
        proj_grad = jnp.concatenate([query_grad_b, key_grad_b, value_grad_b], axis=1)
        grad_qkv = outer_rows(normed, proj_grad)
        grad_bias_query = jnp.sum(query_grad_b.astype(jnp.float32), axis=0)
        grad_bias_value = jnp.sum(value_grad_b.astype(jnp.float32), axis=0)
        normed_grad = times_transposed(proj_grad, qkv_back)
        input_ln_grad, grad_gain_one, grad_shift_one = norm_one_back(normed_grad)
        input_grads.append((middle_grad + input_ln_grad).astype(jnp.bfloat16))
        current = (
            grad_gain_one,
            grad_shift_one,
            grad_qkv,
            grad_bias_query,
            grad_bias_value,
            grad_out,
            grad_bias_out,
            grad_gain_two,
            grad_shift_two,
            grad_up,
            grad_bias_up,
            grad_down,
            grad_bias_down,
        )
        grad_sums = [
            fresh if before is None else before + fresh for before, fresh in zip(grad_sums, current)
        ]
    reduced = lax.psum_scatter(tuple(grad_sums), ("dp", "seq"), scatter_dimension=0, tiled=True)
    return (jnp.stack(outputs_list)[:, None], jnp.stack(input_grads)[:, None]) + tuple(reduced)


def solution(mesh):
    return jax.shard_map(
        body,
        mesh=mesh,
        in_specs=(
            P(None, "dp", "seq", None),
            P(None, "dp", "seq", None),
            P(None, "dp", None, None),
            P(("dp", "seq")),
            P(("dp", "seq")),
            P(("dp", "seq"), None),
            P(("dp", "seq")),
            P(("dp", "seq")),
            P(("dp", "seq"), None),
            P(("dp", "seq")),
            P(("dp", "seq")),
            P(("dp", "seq")),
            P(("dp", "seq"), None),
            P(("dp", "seq")),
            P(("dp", "seq"), None),
            P(("dp", "seq")),
        ),
        out_specs=(
            P(None, "dp", "seq", None),
            P(None, "dp", "seq", None),
            P(("dp", "seq")),
            P(("dp", "seq")),
            P(("dp", "seq"), None),
            P(("dp", "seq")),
            P(("dp", "seq")),
            P(("dp", "seq"), None),
            P(("dp", "seq")),
            P(("dp", "seq")),
            P(("dp", "seq")),
            P(("dp", "seq"), None),
            P(("dp", "seq")),
            P(("dp", "seq"), None),
            P(("dp", "seq")),
        ),
        check_vma=False,
    )
```

profile of v0, /device:TPU:0, one launch (start us, length us, event | category | flops | bytes accessed | tf_op | source)
XLA Modules:
  0.0 1279.3 jit_solution(13797985035123870307)
XLA Ops:
  15.5 42.8 %all-reduce.19 = (bf16[768]{0:T(1024)(128)(2,1)S(1)}, bf16[768]{0:T(1024)(128)(2,1)S(1)}, bf16[768]{0:T(1024)(128)(2,1)S(1)}, bf16[768]{0:T(1024)(128)(2,1)S(1)}...) all-reduce(bf16[768]{0:T(1024)(128)(2,1)S(1)} %dynamic-update-slice, ...), channel_id=1, replica_groups=mesh['dp'=4,'seq'=8] {'dp','seq'}, use_global_device_ids=true, to_apply=%add.1 | all-reduce | flops 9216 | bytes 36864
  61.4 12.4 all-gather.9.cloned.1.call-done
  73.8 2.9 fusion.154
  87.0 34.6 %all-gather.21.cloned.1.call-done = bf16[1024,768]{1,0:T(8,128)(2,1)} async-done(((bf16[128,768]{1,0:T(8,128)(2,1)}), bf16[1024,768]{1,0:T(8,128)(2,1)}) %all-gather.21.cloned.1.call-update) | async-done | bytes 1572880 | tf_op jit(solution)/shard_map/all_gather | solution.py:237
  121.6 2.6 copy.126
  124.3 42.7 %all-gather.23.cloned.1.call-done = bf16[1024,768]{1,0:T(8,128)(2,1)} async-done(((bf16[128,768]{1,0:T(8,128)(2,1)}), bf16[1024,768]{1,0:T(8,128)(2,1)}) %all-gather.23.cloned.1.call-update) | async-done | bytes 1572880 | tf_op jit(solution)/shard_map/all_gather | solution.py:236
  167.0 2.6 copy.128
  169.6 15.7 %while.81 = (s32[]{:T(128)}, f32[128,12,64]{0,2,1:T(8,128)}, f32[12,128]{1,0:T(8,128)S(1)}, bf16[1024,768]{0,1:T(8,128)(2,1)}, s32[2,2]{0,1:T(2,128)}, /*index=5...) while((s32[]{:T(128)}, f32[128,12,64]{0,2,1:T(8,128)}, ...), condition=%wide.region_15.16_spmd.clone, body=%wide.region_11.0_spmd.clone.sunk | while | flops 206512768 | bytes 12520018 | solution.py:86
  169.6 2.4 constant_dynamic-slice_fusion.15
  173.1 1.6 fusion.289
  174.7 2.6 fusion.290
  177.3 2.4 constant_dynamic-slice_fusion.15
  180.9 1.6 fusion.289
  182.5 2.7 fusion.290
  186.4 35.8 %all-gather.15.cloned.1.call-done = bf16[768,768]{1,0:T(8,128)(2,1)} async-done(((bf16[24,768]{1,0:T(8,128)(2,1)}), bf16[768,768]{1,0:T(8,128)(2,1)}) %all-gather.15.cloned.1.call-update) | async-done | bytes 1179664 | tf_op jit(solution)/shard_map/all_gather | solution.py:191
  222.2 1.7 fusion.165
  225.4 42.5 %all-gather.11.cloned.1.call-done = bf16[1024,768]{1,0:T(8,128)(2,1)} async-done(((bf16[128,768]{1,0:T(8,128)(2,1)}), bf16[1024,768]{1,0:T(8,128)(2,1)}) %all-gather.11.cloned.1.call-update) | async-done | bytes 1572880 | tf_op jit(solution)/shard_map/all_gather | solution.py:237
  267.9 2.6 copy.122
  270.5 42.0 %all-gather.13.cloned.1.call-done = bf16[1024,768]{1,0:T(8,128)(2,1)} async-done(((bf16[128,768]{1,0:T(8,128)(2,1)}), bf16[1024,768]{1,0:T(8,128)(2,1)}) %all-gather.13.cloned.1.call-update) | async-done | bytes 1572880 | tf_op jit(solution)/shard_map/all_gather | solution.py:236
  312.5 2.6 copy.124
  315.2 14.2 %while.80 = (s32[]{:T(128)}, f32[128,12,64]{0,2,1:T(8,128)}, f32[12,128]{1,0:T(8,128)S(1)}, bf16[1024,768]{0,1:T(8,128)(2,1)}, s32[2,2]{0,1:T(2,128)}, /*index=5...) while((s32[]{:T(128)}, f32[128,12,64]{0,2,1:T(8,128)}, ...), condition=%wide.region_6.7_spmd.clone, body=%wide.region_2.6_spmd.clone.sunk | while | flops 206512768 | bytes 12233242 | solution.py:86
  315.2 2.3 constant_dynamic-slice_fusion.14
  319.6 2.6 fusion.282
  322.2 2.4 constant_dynamic-slice_fusion.14
  326.7 2.7 fusion.282
  330.6 1.8 fusion.166
  332.6 44.8 %all-gather.17.cloned.1.call-done = bf16[768,3072]{1,0:T(8,128)(2,1)} async-done(((bf16[24,3072]{1,0:T(8,128)(2,1)}), bf16[768,3072]{1,0:T(8,128)(2,1)}) %all-gather.17.cloned.1.call-update) | async-done | bytes 4718608 | tf_op jit(solution)/shard_map/all_gather | solution.py:195
  377.5 8.7 multiply_convert_fusion
  386.2 6.4 multiply_convert_fusion.1
  392.6 49.6 %all-gather.19.cloned.1.call-done = bf16[3072,768]{1,0:T(8,128)(2,1)} async-done(((bf16[96,768]{1,0:T(8,128)(2,1)}), bf16[3072,768]{1,0:T(8,128)(2,1)}) %all-gather.19.cloned.1.call-update) | async-done | bytes 4718608 | tf_op jit(solution)/shard_map/all_gather | solution.py:197
  442.2 5.8 convert_reduce_fusion
  448.0 1.7 fusion.169
  450.6 2.5 convert_reduce_fusion.1
  453.1 2.4 multiply_reduce_fusion.1
  462.0 28.4 %while.83 = (s32[]{:T(128)}, f32[128,12,64]{0,2,1:T(8,128)}, bf16[1024,768]{0,1:T(8,128)(2,1)}, bf16[1024,768]{0,1:T(8,128)(2,1)}, bf16[1024,768]{0,1:T(8,128)(2...) while((s32[]{:T(128)}, f32[128,12,64]{0,2,1:T(8,128)}, ...), condition=%wide.region_35.36_spmd.clone, body=%wide.region_32.35_spmd.clone.sunk | while | flops 510958720 | bytes 62874448 | solution.py:138
  466.5 2.3 fusion.320
  468.8 2.9 fusion.321
  480.6 2.3 fusion.320
  483.0 2.9 fusion.321
  490.3 2.6 copy.153
  494.4 1.6 copy.151
  499.9 28.7 %while.82 = (s32[]{:T(128)}, f32[128,12,64]{0,2,1:T(8,128)}, bf16[1024,768]{0,1:T(8,128)(2,1)}, bf16[1024,768]{0,1:T(8,128)(2,1)}, bf16[1024,768]{0,1:T(8,128)(2...) while((s32[]{:T(128)}, f32[128,12,64]{0,2,1:T(8,128)}, ...), condition=%wide.region_24.25_spmd.clone, body=%wide.region_21.24_spmd.clone.sunk | while | flops 510958720 | bytes 61301528 | solution.py:138
  504.7 2.3 fusion.304
  507.0 2.9 fusion.305
  518.8 2.3 fusion.304
  521.1 2.9 fusion.305
  528.5 2.6 copy.149
  532.6 1.6 copy.147
  535.6 1.9 convolution_add_fusion.5
  539.5 17.6 %reduce-scatter.31.cloned.1.call-done = bf16[128,768]{1,0:T(8,128)(2,1)} async-done(((bf16[1024,768]{1,0:T(8,128)(2,1)}), bf16[128,768]{1,0:T(8,128)(2,1)}) %reduce-scatter.31.cloned.1.call-update) | async-done | bytes 196624
  558.1 66.5 %reduce-scatter.29.cloned.1.call-done = bf16[128,768]{1,0:T(8,128)(2,1)} async-done(((bf16[1024,768]{1,0:T(8,128)(2,1)}), bf16[128,768]{1,0:T(8,128)(2,1)}) %reduce-scatter.29.cloned.1.call-update) | async-done | bytes 196624
  625.7 66.7 %reduce-scatter.27.cloned.1.call-done = bf16[128,768]{1,0:T(8,128)(2,1)} async-done(((bf16[1024,768]{1,0:T(8,128)(2,1)}), bf16[128,768]{1,0:T(8,128)(2,1)}) %reduce-scatter.27.cloned.1.call-update) | async-done | bytes 196624
  693.5 66.6 %reduce-scatter.25.cloned.1.call-done = bf16[128,768]{1,0:T(8,128)(2,1)} async-done(((bf16[1024,768]{1,0:T(8,128)(2,1)}), bf16[128,768]{1,0:T(8,128)(2,1)}) %reduce-scatter.25.cloned.1.call-update) | async-done | bytes 196624
  762.6 4.2 convolution_add_fusion
  768.1 1.5 fusion.158
  769.6 5.2 convolution_add_fusion.2
  777.5 5.1 convolution_add_fusion.1
  792.3 3.2 fusion.88
  795.6 3.3 fusion.89
  803.5 40.7 %all-reduce.18 = (f32[768]{0:T(1024)S(1)}, f32[768]{0:T(1024)S(1)}, f32[768]{0:T(1024)S(1)}, f32[768]{0:T(1024)S(1)}, f32[768]{0:T(1024)S(1)}, /*index=5*/f32[76...) all-reduce(f32[768]{0:T(1024)S(1)} %add.789, ...), channel_id=6, replica_groups=mesh['dp'=4,'seq'=8] {'dp','seq'}, use_global_device_ids=true, to_apply=%region_42.43.clone | all-reduce | flops 9216 | bytes 73728
  850.7 14.1 %reduce-scatter.19.cloned.1.call-done = f32[24,768]{1,0:T(8,128)} async-done(((f32[768,768]{1,0:T(8,128)}), f32[24,768]{1,0:T(8,128)}) %reduce-scatter.19.cloned.1.call-update) | async-done | bytes 73744 | tf_op jit(solution)/shard_map/reduce_scatter | solution.py:336
  864.9 124.7 %reduce-scatter.17.cloned.1.call-done = f32[24,2304]{1,0:T(8,128)} async-done(((f32[768,2304]{1,0:T(8,128)}), f32[24,2304]{1,0:T(8,128)}) %reduce-scatter.17.cloned.1.call-update) | async-done | bytes 221200 | tf_op jit(solution)/shard_map/reduce_scatter | solution.py:336
  989.6 141.5 %reduce-scatter.21.cloned.1.call-done = f32[24,3072]{1,0:T(8,128)} async-done(((f32[768,3072]{1,0:T(8,128)}), f32[24,3072]{1,0:T(8,128)}) %reduce-scatter.21.cloned.1.call-update) | async-done | bytes 294928 | tf_op jit(solution)/shard_map/reduce_scatter | solution.py:336
  1131.1 141.5 %reduce-scatter.23.cloned.1.call-done = f32[96,768]{1,0:T(8,128)} async-done(((f32[3072,768]{1,0:T(8,128)}), f32[96,768]{1,0:T(8,128)}) %reduce-scatter.23.cloned.1.call-update) | async-done | bytes 294928 | tf_op jit(solution)/shard_map/reduce_scatter | solution.py:336
  (535 shorter events, 114.4 us)
Async XLA Ops:
  7.2 66.6 %all-gather.9.cloned.1.call-start = ((), (), s32[]{:S(2)}) async-start(), calls=%async_computation.8 | async-start | bytes 3649536 | tf_op jit(solution)/shard_map/all_gather | solution.py:188
  7.9 113.7 %all-gather.21.cloned.1.call-start = ((), (), s32[]{:S(2)}) async-start(), calls=%async_computation.14 | async-start | bytes 1769472 | tf_op jit(solution)/shard_map/all_gather | solution.py:237
  58.3 18.4 %copy-start.73 = (f32[768]{0:T(1024)}, f32[768]{0:T(1024)S(1)}, u32[]{:S(2)}) copy-start(f32[768]{0:T(1024)S(1)} %convert_element_type.265) | copy-start | bytes 9220
  58.3 18.4 %copy-start.68 = (f32[768]{0:T(1024)}, f32[768]{0:T(1024)S(1)}, u32[]{:S(2)}) copy-start(f32[768]{0:T(1024)S(1)} %convert_element_type.264) | copy-start | bytes 9220
  59.5 14.2 %copy-start.83 = (f32[128]{0:T(128)}, f32[128]{0:T(128)S(1)}, u32[]{:S(2)}) copy-start(f32[128]{0:T(128)S(1)} %get-tuple-element.1592) | copy-start | bytes 1540
  59.5 17.2 %copy-start.80 = (f32[128]{0:T(128)}, f32[128]{0:T(128)S(1)}, u32[]{:S(2)}) copy-start(f32[128]{0:T(128)S(1)} %get-tuple-element.1593) | copy-start | bytes 1540
  60.8 15.9 %copy-start.115 = (f32[128]{0:T(128)}, f32[128]{0:T(128)S(1)}, u32[]{:S(2)}) copy-start(f32[128]{0:T(128)S(1)} %get-tuple-element.1423) | copy-start | bytes 1540
  61.4 12.4 copy-start.101
  61.4 15.4 %copy-start.94 = (f32[128]{0:T(128)}, f32[128]{0:T(128)S(1)}, u32[]{:S(2)}) copy-start(f32[128]{0:T(128)S(1)} %fusion.142) | copy-start | bytes 1540
  61.4 15.4 %copy-start.7 = (bf16[2,1,128,768]{3,2,1,0:T(8,128)(2,1)S(1)}, bf16[2,1,128,768]{3,2,1,0:T(8,128)(2,1)}, u32[]{:S(2)}) copy-start(bf16[2,1,128,768]{3,2,1,0:T(8,128)(2,1)} %param.24) | copy-start | bytes 1179652
  73.7 3.2 copy-start.22
  77.6 6.0 copy-start.112
  78.5 88.5 %all-gather.23.cloned.1.call-start = ((), (), s32[]{:S(2)}) async-start(), calls=%async_computation.15 | async-start | bytes 1769472 | tf_op jit(solution)/shard_map/all_gather | solution.py:236
  79.3 142.9 %all-gather.15.cloned.1.call-start = ((), (), s32[]{:S(2)}) async-start(), calls=%async_computation.11 | async-start | bytes 1216512 | tf_op jit(solution)/shard_map/all_gather | solution.py:191
  79.9 188.1 %all-gather.11.cloned.1.call-start = ((), (), s32[]{:S(2)}) async-start(), calls=%async_computation.9 | async-start | bytes 1769472 | tf_op jit(solution)/shard_map/all_gather | solution.py:237
  80.4 232.1 %all-gather.13.cloned.1.call-start = ((), (), s32[]{:S(2)}) async-start(), calls=%async_computation.10 | async-start | bytes 1769472 | tf_op jit(solution)/shard_map/all_gather | solution.py:236
  81.2 296.2 %all-gather.17.cloned.1.call-start = ((), (), s32[]{:S(2)}) async-start(), calls=%async_computation.12 | async-start | bytes 4866048 | tf_op jit(solution)/shard_map/all_gather | solution.py:195
  82.0 360.3 %all-gather.19.cloned.1.call-start = ((), (), s32[]{:S(2)}) async-start(), calls=%async_computation.13 | async-start | bytes 4866048 | tf_op jit(solution)/shard_map/all_gather | solution.py:197
  82.7 474.3 %reduce-scatter.31.cloned.1.call-start = ((), (), s32[]{:S(2)}) async-start(), calls=%async_computation.23 | async-start | bytes 1769472
  185.2 85.3 %copy-start.4 = (bf16[128,12,64]{0,2,1:T(8,128)(2,1)}, bf16[128,12,64]{0,2,1:T(8,128)(2,1)S(1)}, u32[]{:S(2)}) copy-start(bf16[128,12,64]{0,2,1:T(8,128)(2,1)S(1)} %get-tuple-element.2051) | copy-start | bytes 589828
  186.4 84.2 %copy-start.52 = (bf16[128,12,64]{0,2,1:T(8,128)(2,1)}, bf16[128,12,64]{0,2,1:T(8,128)(2,1)S(1)}, u32[]{:S(2)}) copy-start(bf16[128,12,64]{0,2,1:T(8,128)(2,1)S(1)} %fusion.137) | copy-start | bytes 589828
  315.2 15.4 %copy-start.78 = (f32[768]{0:T(1024)S(1)}, f32[768]{0:T(1024)}, u32[]{:S(2)}) copy-start(f32[768]{0:T(1024)} %convert_element_type.273) | copy-start | bytes 9220
  329.4 3.2 copy-start.117
  329.4 48.1 %copy-start.27 = (f32[128,768]{1,0:T(8,128)S(1)}, f32[128,768]{1,0:T(8,128)}, u32[]{:S(2)}) copy-start(f32[128,768]{1,0:T(8,128)} %copy-done.26) | copy-start | bytes 1179652
  329.4 48.1 %copy-start.71 = (f32[768]{0:T(1024)S(1)}, f32[768]{0:T(1024)}, u32[]{:S(2)}) copy-start(f32[768]{0:T(1024)} %convert_element_type.274) | copy-start | bytes 9220
  329.4 48.0 %copy-start.76 = (f32[768]{0:T(1024)S(1)}, f32[768]{0:T(1024)}, u32[]{:S(2)}) copy-start(f32[768]{0:T(1024)} %convert_element_type.275) | copy-start | bytes 9220
  329.4 48.0 %copy-start.97 = (f32[3072]{0:T(1024)S(1)}, f32[3072]{0:T(1024)}, u32[]{:S(2)}) copy-start(f32[3072]{0:T(1024)} %convert_element_type.277) | copy-start | bytes 36868
  329.4 48.0 %copy-start.99 = (f32[128]{0:T(128)S(1)}, f32[128]{0:T(128)}, u32[]{:S(2)}) copy-start(f32[128]{0:T(128)} %copy-done.98) | copy-start | bytes 1540
  330.5 55.6 %copy-start.56 = (bf16[128,12,64]{0,2,1:T(8,128)(2,1)}, bf16[128,12,64]{0,2,1:T(8,128)(2,1)S(1)}, u32[]{:S(2)}) copy-start(bf16[128,12,64]{0,2,1:T(8,128)(2,1)S(1)} %fusion.136) | copy-start | bytes 589828
  332.4 123.2 %copy-start.16 = (f32[128,768]{1,0:T(8,128)}, f32[128,768]{1,0:T(8,128)S(1)}, u32[]{:S(2)}) copy-start(f32[128,768]{1,0:T(8,128)S(1)} %get-tuple-element.1584) | copy-start | bytes 1179652
  332.4 123.2 %copy-start.92 = (f32[128]{0:T(128)}, f32[128]{0:T(128)S(1)}, u32[]{:S(2)}) copy-start(f32[128]{0:T(128)S(1)} %broadcast_multiply_fusion.2) | copy-start | bytes 1540
  332.6 123.0 %copy-start.106 = (f32[128]{0:T(128)}, f32[128]{0:T(128)S(1)}, u32[]{:S(2)}) copy-start(f32[128]{0:T(128)S(1)} %fusion.145) | copy-start | bytes 1540
  332.6 122.9 %copy-start.104 = (f32[128]{0:T(128)}, f32[128]{0:T(128)S(1)}, u32[]{:S(2)}) copy-start(f32[128]{0:T(128)S(1)} %fusion.143) | copy-start | bytes 1540
  377.5 8.7 copy-start.14
  386.2 56.1 %copy-start.41 = (bf16[2,1,128,768]{3,2,1,0:T(8,128)(2,1)S(1)}, bf16[2,1,128,768]{3,2,1,0:T(8,128)(2,1)}, u32[]{:S(2)}) copy-start(bf16[2,1,128,768]{3,2,1,0:T(8,128)(2,1)} %param.25) | copy-start | bytes 1179652
  442.2 5.8 copy-start.15
  442.2 7.5 copy-start.118
  442.2 7.5 copy-start.119
  483.0 2.9 copy-start.19
  493.0 131.7 %reduce-scatter.29.cloned.1.call-start = ((), (), s32[]{:S(2)}) async-start(), calls=%async_computation.22 | async-start | bytes 1769472
  497.1 195.4 %reduce-scatter.27.cloned.1.call-start = ((), (), s32[]{:S(2)}) async-start(), calls=%async_computation.21 | async-start | bytes 1769472
  521.1 2.9 copy-start.21
  531.2 229.0 %reduce-scatter.25.cloned.1.call-start = ((), (), s32[]{:S(2)}) async-start(), calls=%async_computation.20 | async-start | bytes 1769472
  534.2 330.7 %reduce-scatter.19.cloned.1.call-start = ((), (), s32[]{:S(2)}) async-start(), calls=%async_computation.17 | async-start | bytes 2433024 | tf_op jit(solution)/shard_map/reduce_scatter | solution.py:336
  537.5 223.7 %copy-start.8 = (bf16[2,1,128,768]{3,2,1,0:T(8,128)(2,1)S(1)}, bf16[2,1,128,768]{3,2,1,0:T(8,128)(2,1)}, u32[]{:S(2)}) copy-start(bf16[2,1,128,768]{3,2,1,0:T(8,128)(2,1)} %param.24) | copy-start | bytes 1179652
  537.6 223.7 %copy-start.69 = (f32[768]{0:T(1024)S(1)}, f32[768]{0:T(1024)}, u32[]{:S(2)}) copy-start(f32[768]{0:T(1024)} %copy-done.68) | copy-start | bytes 9220
  537.6 223.7 %copy-start.74 = (f32[768]{0:T(1024)S(1)}, f32[768]{0:T(1024)}, u32[]{:S(2)}) copy-start(f32[768]{0:T(1024)} %copy-done.73) | copy-start | bytes 9220
  537.6 223.7 %copy-start.81 = (f32[128]{0:T(128)S(1)}, f32[128]{0:T(128)}, u32[]{:S(2)}) copy-start(f32[128]{0:T(128)} %copy-done.80) | copy-start | bytes 1540
  537.6 223.7 %copy-start.95 = (f32[128]{0:T(128)S(1)}, f32[128]{0:T(128)}, u32[]{:S(2)}) copy-start(f32[128]{0:T(128)} %copy-done.94) | copy-start | bytes 1540
  537.6 452.0 %reduce-scatter.17.cloned.1.call-start = ((), (), s32[]{:S(2)}) async-start(), calls=%async_computation.16 | async-start | bytes 7299072 | tf_op jit(solution)/shard_map/reduce_scatter | solution.py:336
  538.7 223.9 %copy-start.62 = (bf16[128,12,64]{0,2,1:T(8,128)(2,1)}, bf16[128,12,64]{0,2,1:T(8,128)(2,1)S(1)}, u32[]{:S(2)}) copy-start(bf16[128,12,64]{0,2,1:T(8,128)(2,1)S(1)} %get-tuple-element.1526) | copy-start | bytes 589828
  539.5 223.1 %copy-start.66 = (bf16[128,12,64]{0,2,1:T(8,128)(2,1)}, bf16[128,12,64]{0,2,1:T(8,128)(2,1)S(1)}, u32[]{:S(2)}) copy-start(bf16[128,12,64]{0,2,1:T(8,128)(2,1)S(1)} %get-tuple-element.1528) | copy-start | bytes 589828
  625.7 136.8 %copy-start.60 = (bf16[128,768]{0,1:T(8,128)(2,1)}, bf16[128,768]{0,1:T(8,128)(2,1)S(1)}, u32[]{:S(2)}) copy-start(bf16[128,768]{0,1:T(8,128)(2,1)S(1)} %copy.152) | copy-start | bytes 589828
  766.9 364.2 %reduce-scatter.21.cloned.1.call-start = ((), (), s32[]{:S(2)}) async-start(), calls=%async_computation.18 | async-start | bytes 9732096 | tf_op jit(solution)/shard_map/reduce_scatter | solution.py:336
  774.8 497.8 %reduce-scatter.23.cloned.1.call-start = ((), (), s32[]{:S(2)}) async-start(), calls=%async_computation.19 | async-start | bytes 9732096 | tf_op jit(solution)/shard_map/reduce_scatter | solution.py:336
  782.5 6.5 copy-start.86
  792.3 3.2 copy-start.79
  795.5 4.2 copy-start.23
  795.5 4.2 copy-start.61
  795.5 4.2 copy-start.63
  802.6 46.9 %copy-start.44 = (f32[128,768]{1,0:T(8,128)S(1)}, f32[128,768]{1,0:T(8,128)}, u32[]{:S(2)}) copy-start(f32[128,768]{1,0:T(8,128)} %copy-done.43) | copy-start | bytes 1179652
  802.6 46.9 %copy-start.46 = (f32[128,768]{1,0:T(8,128)S(1)}, f32[128,768]{1,0:T(8,128)}, u32[]{:S(2)}) copy-start(f32[128,768]{1,0:T(8,128)} %copy-done.45) | copy-start | bytes 1179652
  802.6 46.9 %copy-start.109 = (f32[128]{0:T(128)S(1)}, f32[128]{0:T(128)}, u32[]{:S(2)}) copy-start(f32[128]{0:T(128)} %copy-done.108) | copy-start | bytes 1540
  802.7 46.9 %copy-start.111 = (f32[128]{0:T(128)S(1)}, f32[128]{0:T(128)}, u32[]{:S(2)}) copy-start(f32[128]{0:T(128)} %copy-done.110) | copy-start | bytes 1540
  (92 other events, 144.1 us)
Sparse Core Ops, SparseCore 0:
  10.9 62.7 all-gather.8
  78.6 42.9 all-gather.20
  124.4 42.5 all-gather.22
  169.7 52.4 all-gather.14
  224.8 43.0 all-gather.10
  270.0 42.5 all-gather.12
  315.4 61.9 all-gather.16
  380.4 61.8 all-gather.18
  493.1 63.8 reduce-scatter.30
  560.3 64.2 reduce-scatter.28
  628.1 64.2 reduce-scatter.26
  695.7 64.3 reduce-scatter.24
  766.0 98.8 reduce-scatter.18
  871.0 118.5 reduce-scatter.16
  995.9 135.1 reduce-scatter.20
  1137.4 135.1 reduce-scatter.22
where the time goes:
time: 1290 us; the launch traced here: 1280 us
  waiting for transfers between devices  947 us (73%)
  matrix products  110 us (9%)
  local copies, waits for them, and re-layouts  94.1 us (7%)
  blocking collectives  83.5 us (6%)
  other arithmetic  26.8 us (2%)
  between operations  15.6 us (1%)
    reduce_scatter x4, waiting for transfers between devices, body(): lax.psum_scatter(tuple(grad_sums), ('dp', 'seq'), scatter_dimension=0, ti...  422 us
    unnamed x20, waiting for transfers between devices  221 us
    all_gather x2, waiting for transfers between devices, body(): lax.all_gather(keys_now, 'seq', axis=0, tiled=True)  84.7 us
    unnamed x2, blocking collectives  83.5 us
    all_gather x2, waiting for transfers between devices, body(): lax.all_gather(values_now, 'seq', axis=0, tiled=True)  77.2 us
    all_gather x1, waiting for transfers between devices, body(): lax.all_gather(shards[11], ('dp', 'seq'), axis=0, tiled=True)  49.6 us
    unnamed x241, local copies, waits for them, and re-layouts  47.1 us
    all_gather x1, waiting for transfers between devices, body(): lax.all_gather(shards[9], ('dp', 'seq'), axis=0, tiled=True)  44.8 us
  transfers between devices with their start and end apart: 16, of which 16 were waited for; matrix products, arithmetic and copies ran while one was open for 13% of the time, Pallas kernels for 0%

commit v1 on v0

--- a/solution.py
+++ b/solution.py
@@ -7,6 +7,9 @@
 HEADS = 12
 HEAD = 64
 EPSILON = 1e-05
+supply_all_orders = lambda local: jnp.concatenate(
+    lax.all_to_all(jnp.stack([local for _ in range(lax.axis_size("seq"))]), "seq", 0, 0), axis=0
+)
 
 
 def layer_norm(values, ln_gain, ln_shift):
@@ -232,10 +235,7 @@
         fold_keys = forward_fold(query_heads, query_pos, seq_bounds)
         weighted, totals = fold_keys(
             start_sums,
-            (
-                lax.all_gather(keys_now, "seq", axis=0, tiled=True),
-                lax.all_gather(values_now, "seq", axis=0, tiled=True),
-            ),
+            (lax.all_gather(keys_now, "seq", axis=0, tiled=True), supply_all_orders(values_now)),
             jnp.int32(0),
         )
         attended = weighted / totals.T[:, :, None]

time: 1290 us -> 1270 us (0.984)
  waiting for transfers between devices: 947 us -> 896 us
  matrix products: 110 us -> 126 us
    all_gather x2, waiting for transfers between devices: 77.2 us -> 26.8 us  [body(): lax.all_gather(values_now, 'seq', axis=0, tiled=True)]
    all_to_all x0 -> x2, waiting for transfers between devices: none -> 48.6 us  [lax.all_to_all(jnp.stack([local for _ in range(lax.axis_size('seq'))]), '...]
    all_gather x2, waiting for transfers between devices: 84.7 us -> 39.9 us  [body(): lax.all_gather(keys_now, 'seq', axis=0, tiled=True)]
    dynamic_slice x4 -> x16, local copies, waits for them, and re-layouts: 4.74 us -> 19.2 us  [inner_step(): lax.dynamic_slice_in_dim(value_piece, offset, step_len, 0)]
    unnamed x241 -> x273, local copies, waits for them, and re-layouts: 47.1 us -> 41.5 us
  transfers between devices with their start and end apart: 16 -> 18, of which waited for: 16 -> 15; matrix products, arithmetic and copies ran while one was open for 13% -> 18% of each run, Pallas kernels for 0% -> 0%
where the time goes in v1:
time: 1270 us; the launch traced here: 1260 us
  waiting for transfers between devices  896 us (71%)
  matrix products  126 us (10%)
  local copies, waits for them, and re-layouts  103 us (8%)
  blocking collectives  83.5 us (7%)
  other arithmetic  26.7 us (2%)
  between operations  15.8 us (1%)
    reduce_scatter x4, waiting for transfers between devices, body(): lax.psum_scatter(tuple(grad_sums), ('dp', 'seq'), scatter_dimension=0, ti...  422 us
    unnamed x20, waiting for transfers between devices  218 us
    unnamed x2, blocking collectives  83.5 us
    all_gather x1, waiting for transfers between devices, body(): lax.all_gather(shards[11], ('dp', 'seq'), axis=0, tiled=True)  49.3 us
    all_to_all x2, waiting for transfers between devices, lax.all_to_all(jnp.stack([local for _ in range(lax.axis_size('seq'))]), '...  48.6 us
    all_gather x1, waiting for transfers between devices, body(): lax.all_gather(shards[9], ('dp', 'seq'), axis=0, tiled=True)  43.1 us
    unnamed x273, local copies, waits for them, and re-layouts  41.5 us
    all_gather x2, waiting for transfers between devices, body(): lax.all_gather(keys_now, 'seq', axis=0, tiled=True)  39.9 us
  transfers between devices with their start and end apart: 18, of which 15 were waited for; matrix products, arithmetic and copies ran while one was open for 18% of the time, Pallas kernels for 0%

profile of v1, /device:TPU:0, one launch (start us, length us, event | category | flops | bytes accessed | tf_op | source)
XLA Modules:
  0.0 1261.6 jit_solution(16376697008124305342)
XLA Ops:
  15.5 42.8 %all-reduce.19 = (bf16[768]{0:T(1024)(128)(2,1)S(1)}, bf16[768]{0:T(1024)(128)(2,1)S(1)}, bf16[768]{0:T(1024)(128)(2,1)S(1)}, bf16[768]{0:T(1024)(128)(2,1)S(1)}...) all-reduce(bf16[768]{0:T(1024)(128)(2,1)S(1)} %dynamic-update-slice, ...), channel_id=1, replica_groups=mesh['dp'=4,'seq'=8] {'dp','seq'}, use_global_device_ids=true, to_apply=%add.1 | all-reduce | flops 9216 | bytes 36864
  60.8 12.9 %all-gather.9.cloned.1.call-done = bf16[768,2304]{1,0:T(8,128)(2,1)} async-done(((bf16[24,2304]{1,0:T(8,128)(2,1)}), bf16[768,2304]{1,0:T(8,128)(2,1)}) %all-gather.9.cloned.1.call-update) | async-done | bytes 3538960 | tf_op jit(solution)/shard_map/all_gather | solution.py:191
  73.7 2.8 fusion.154
  78.2 2.7 fusion.151
  85.0 4.4 all-to-all-start.1
  93.8 48.5 %all-to-all-done.1 = bf16[8,128,768]{1,2,0:T(8,128)(2,1)S(1)} async-done(((bf16[8,128,768]{1,2,0:T(8,128)(2,1)}), bf16[8,128,768]{1,2,0:T(8,128)(2,1)S(1)}, u32[]{:S(2)}, u32[]{:S(2)}) %all-to-all-start.1) | async-done | bytes 1572896 | tf_op jit(solution)/shard_map/all_to_all | solution.py:11
  143.7 4.3 all-to-all-start
  149.8 1.7 copy.162
  151.6 18.8 %while.81 = (s32[]{:T(128)}, f32[128,12,64]{0,2,1:T(8,128)}, f32[12,128]{1,0:T(8,128)S(1)}, bf16[1024,768]{1,0:T(8,128)(2,1)}, s32[2,2]{0,1:T(2,128)}, /*index=5...) while((s32[]{:T(128)}, f32[128,12,64]{0,2,1:T(8,128)}, ...), condition=%wide.region_15.16_spmd.clone, body=%wide.region_11.0_spmd.clone.sunk | while | flops 206512768 | bytes 14092886 | solution.py:89
  154.4 3.2 fusion.289
  157.6 3.4 fusion.290
  163.7 3.2 fusion.289
  166.9 3.4 fusion.290
  171.8 35.5 %all-gather.13.cloned.1.call-done = bf16[768,768]{1,0:T(8,128)(2,1)} async-done(((bf16[24,768]{1,0:T(8,128)(2,1)}), bf16[768,768]{1,0:T(8,128)(2,1)}) %all-gather.13.cloned.1.call-update) | async-done | bytes 1179664 | tf_op jit(solution)/shard_map/all_gather | solution.py:194
  207.2 1.7 fusion.165
  210.4 2.6 copy.152
  213.1 39.9 %all-gather.11.cloned.1.call-done = bf16[1024,768]{1,0:T(8,128)(2,1)} async-done(((bf16[128,768]{1,0:T(8,128)(2,1)}), bf16[1024,768]{1,0:T(8,128)(2,1)}) %all-gather.11.cloned.1.call-update) | async-done | bytes 1572880 | tf_op jit(solution)/shard_map/all_gather | solution.py:238
  252.9 1.7 copy.156
  254.7 16.1 %while.80 = (s32[]{:T(128)}, f32[128,12,64]{0,2,1:T(8,128)}, f32[12,128]{1,0:T(8,128)S(1)}, bf16[1024,768]{1,0:T(8,128)(2,1)}, s32[2,2]{0,1:T(2,128)S(1)}, /*ind...) while((s32[]{:T(128)}, f32[128,12,64]{0,2,1:T(8,128)}, ...), condition=%wide.region_6.7_spmd.clone, body=%wide.region_2.6_spmd.clone.sunk | while | flops 206512768 | bytes 13806110 | solution.py:89
  256.7 2.6 fusion.281
  259.3 3.4 fusion.282
  264.7 2.6 fusion.281
  267.3 3.4 fusion.282
  272.4 1.8 fusion.166
  274.5 43.1 %all-gather.15.cloned.1.call-done = bf16[768,3072]{1,0:T(8,128)(2,1)} async-done(((bf16[24,3072]{1,0:T(8,128)(2,1)}), bf16[768,3072]{1,0:T(8,128)(2,1)}) %all-gather.15.cloned.1.call-update) | async-done | bytes 4718608 | tf_op jit(solution)/shard_map/all_gather | solution.py:198
  317.7 8.7 multiply_convert_fusion
  326.4 6.6 multiply_convert_fusion.1
  333.0 49.3 %all-gather.17.cloned.1.call-done = bf16[3072,768]{1,0:T(8,128)(2,1)} async-done(((bf16[96,768]{1,0:T(8,128)(2,1)}), bf16[3072,768]{1,0:T(8,128)(2,1)}) %all-gather.17.cloned.1.call-update) | async-done | bytes 4718608 | tf_op jit(solution)/shard_map/all_gather | solution.py:200
  382.3 5.8 convert_reduce_fusion
  388.0 1.7 fusion.169
  390.7 2.5 convert_reduce_fusion.1
  394.1 2.4 multiply_reduce_fusion.1
  400.8 26.8 %all-gather.23.cloned.1.call-done = bf16[1024,768]{1,0:T(8,128)(2,1)} async-done(((bf16[128,768]{1,0:T(8,128)(2,1)}), bf16[1024,768]{1,0:T(8,128)(2,1)}) %all-gather.23.cloned.1.call-update) | async-done | bytes 1572880 | tf_op jit(solution)/shard_map/all_gather | solution.py:295
  430.3 36.6 %while.83 = (s32[]{:T(128)}, f32[128,12,64]{0,2,1:T(8,128)}, bf16[1024,768]{0,1:T(8,128)(2,1)}, bf16[1024,768]{0,1:T(8,128)(2,1)}, bf16[1024,768]{0,1:T(8,128)(2...) while((s32[]{:T(128)}, f32[128,12,64]{0,2,1:T(8,128)}, ...), condition=%wide.region_35.36_spmd.clone, body=%wide.region_32.35_spmd.clone.sunk | while | flops 510958720 | bytes 70738792 | solution.py:141
  434.3 2.3 copy.200
  437.8 3.5 fusion.320
  441.3 2.9 fusion.321
  452.6 2.3 copy.200
  456.0 3.5 fusion.320
  459.5 2.9 fusion.321
  466.9 2.7 copy.187
  476.5 36.6 %while.82 = (s32[]{:T(128)}, f32[128,12,64]{0,2,1:T(8,128)}, bf16[1024,768]{0,1:T(8,128)(2,1)}, bf16[1024,768]{0,1:T(8,128)(2,1)}, bf16[1024,768]{0,1:T(8,128)(2...) while((s32[]{:T(128)}, f32[128,12,64]{0,2,1:T(8,128)}, ...), condition=%wide.region_24.25_spmd.clone, body=%wide.region_21.24_spmd.clone.sunk | while | flops 510958720 | bytes 69165880 | solution.py:141
  480.8 2.3 copy.199
  484.2 3.4 fusion.304
  487.6 2.9 fusion.305
  498.9 2.3 copy.199
  502.3 3.4 fusion.304
  505.7 2.9 fusion.305
  513.1 2.6 copy.183
  520.1 1.9 convolution_add_fusion.5
  524.0 15.7 %reduce-scatter.31.cloned.1.call-done = bf16[128,768]{1,0:T(8,128)(2,1)} async-done(((bf16[1024,768]{1,0:T(8,128)(2,1)}), bf16[128,768]{1,0:T(8,128)(2,1)}) %reduce-scatter.31.cloned.1.call-update) | async-done | bytes 196624
  540.8 66.5 %reduce-scatter.29.cloned.1.call-done = bf16[128,768]{1,0:T(8,128)(2,1)} async-done(((bf16[1024,768]{1,0:T(8,128)(2,1)}), bf16[128,768]{1,0:T(8,128)(2,1)}) %reduce-scatter.29.cloned.1.call-update) | async-done | bytes 196624
  608.4 66.6 %reduce-scatter.27.cloned.1.call-done = bf16[128,768]{1,0:T(8,128)(2,1)} async-done(((bf16[1024,768]{1,0:T(8,128)(2,1)}), bf16[128,768]{1,0:T(8,128)(2,1)}) %reduce-scatter.27.cloned.1.call-update) | async-done | bytes 196624
  676.1 66.5 %reduce-scatter.25.cloned.1.call-done = bf16[128,768]{1,0:T(8,128)(2,1)} async-done(((bf16[1024,768]{1,0:T(8,128)(2,1)}), bf16[128,768]{1,0:T(8,128)(2,1)}) %reduce-scatter.25.cloned.1.call-update) | async-done | bytes 196624
  745.1 4.2 convolution_add_fusion
  752.1 5.2 convolution_add_fusion.2
  759.9 5.1 convolution_add_fusion.1
  774.8 3.2 fusion.88
  778.0 3.3 fusion.89
  786.0 40.7 %all-reduce.18 = (f32[768]{0:T(1024)S(1)}, f32[768]{0:T(1024)S(1)}, f32[768]{0:T(1024)S(1)}, f32[768]{0:T(1024)S(1)}, f32[768]{0:T(1024)S(1)}, /*index=5*/f32[76...) all-reduce(f32[768]{0:T(1024)S(1)} %add.789, ...), channel_id=6, replica_groups=mesh['dp'=4,'seq'=8] {'dp','seq'}, use_global_device_ids=true, to_apply=%region_42.43.clone | all-reduce | flops 9216 | bytes 73728
  833.2 14.1 %reduce-scatter.19.cloned.1.call-done = f32[24,768]{1,0:T(8,128)} async-done(((f32[768,768]{1,0:T(8,128)}), f32[24,768]{1,0:T(8,128)}) %reduce-scatter.19.cloned.1.call-update) | async-done | bytes 73744 | tf_op jit(solution)/shard_map/reduce_scatter | solution.py:336
  847.2 124.7 %reduce-scatter.17.cloned.1.call-done = f32[24,2304]{1,0:T(8,128)} async-done(((f32[768,2304]{1,0:T(8,128)}), f32[24,2304]{1,0:T(8,128)}) %reduce-scatter.17.cloned.1.call-update) | async-done | bytes 221200 | tf_op jit(solution)/shard_map/reduce_scatter | solution.py:336
  972.0 141.4 %reduce-scatter.21.cloned.1.call-done = f32[24,3072]{1,0:T(8,128)} async-done(((f32[768,3072]{1,0:T(8,128)}), f32[24,3072]{1,0:T(8,128)}) %reduce-scatter.21.cloned.1.call-update) | async-done | bytes 294928 | tf_op jit(solution)/shard_map/reduce_scatter | solution.py:336
  1113.4 141.5 %reduce-scatter.23.cloned.1.call-done = f32[96,768]{1,0:T(8,128)} async-done(((f32[3072,768]{1,0:T(8,128)}), f32[96,768]{1,0:T(8,128)}) %reduce-scatter.23.cloned.1.call-update) | async-done | bytes 294928 | tf_op jit(solution)/shard_map/reduce_scatter | solution.py:336
  (597 shorter events, 128.8 us)
Async XLA Ops:
  7.2 66.6 %all-gather.9.cloned.1.call-start = ((), (), s32[]{:S(2)}) async-start(), calls=%async_computation.10 | async-start | bytes 3649536 | tf_op jit(solution)/shard_map/all_gather | solution.py:191
  7.9 141.9 %all-gather.19.cloned.1.call-start = ((), (), s32[]{:S(2)}) async-start(), calls=%async_computation.15 | async-start | bytes 1769472 | tf_op jit(solution)/shard_map/all_gather | solution.py:238
  58.3 19.8 %copy-start.81 = (f32[768]{0:T(1024)}, f32[768]{0:T(1024)S(1)}, u32[]{:S(2)}) copy-start(f32[768]{0:T(1024)S(1)} %convert_element_type.265) | copy-start | bytes 9220
  58.3 19.8 %copy-start.75 = (f32[768]{0:T(1024)}, f32[768]{0:T(1024)S(1)}, u32[]{:S(2)}) copy-start(f32[768]{0:T(1024)S(1)} %convert_element_type.264) | copy-start | bytes 9220
  59.5 17.1 %copy-start.91 = (f32[128]{0:T(128)}, f32[128]{0:T(128)S(1)}, u32[]{:S(2)}) copy-start(f32[128]{0:T(128)S(1)} %get-tuple-element.1641) | copy-start | bytes 1540
  59.5 18.6 %copy-start.88 = (f32[128]{0:T(128)}, f32[128]{0:T(128)S(1)}, u32[]{:S(2)}) copy-start(f32[128]{0:T(128)S(1)} %get-tuple-element.1642) | copy-start | bytes 1540
  60.8 15.8 %copy-start.129 = (f32[128]{0:T(128)}, f32[128]{0:T(128)S(1)}, u32[]{:S(2)}) copy-start(f32[128]{0:T(128)S(1)} %get-tuple-element.1477) | copy-start | bytes 1540
  60.8 17.3 %copy-start.131 = (f32[128]{0:T(128)}, f32[128]{0:T(128)S(1)}, u32[]{:S(2)}) copy-start(f32[128]{0:T(128)S(1)} %get-tuple-element.1476) | copy-start | bytes 1540
  60.8 15.8 %copy-start.111 = (f32[128]{0:T(128)}, f32[128]{0:T(128)S(1)}, u32[]{:S(2)}) copy-start(f32[128]{0:T(128)S(1)} %fusion.144) | copy-start | bytes 1540
  60.8 17.3 %copy-start.9 = (bf16[2,1,128,768]{3,2,1,0:T(8,128)(2,1)S(1)}, bf16[2,1,128,768]{3,2,1,0:T(8,128)(2,1)}, u32[]{:S(2)}) copy-start(bf16[2,1,128,768]{3,2,1,0:T(8,128)(2,1)} %param.24) | copy-start | bytes 1179652
  77.3 129.9 %all-gather.13.cloned.1.call-start = ((), (), s32[]{:S(2)}) async-start(), calls=%async_computation.12 | async-start | bytes 1216512 | tf_op jit(solution)/shard_map/all_gather | solution.py:194
  78.0 174.9 %all-gather.11.cloned.1.call-start = ((), (), s32[]{:S(2)}) async-start(), calls=%async_computation.11 | async-start | bytes 1769472 | tf_op jit(solution)/shard_map/all_gather | solution.py:238
  81.6 236.0 %all-gather.15.cloned.1.call-start = ((), (), s32[]{:S(2)}) async-start(), calls=%async_computation.13 | async-start | bytes 4866048 | tf_op jit(solution)/shard_map/all_gather | solution.py:198
  82.2 300.1 %all-gather.17.cloned.1.call-start = ((), (), s32[]{:S(2)}) async-start(), calls=%async_computation.14 | async-start | bytes 4866048 | tf_op jit(solution)/shard_map/all_gather | solution.py:200
  82.8 344.8 %all-gather.23.cloned.1.call-start = ((), (), s32[]{:S(2)}) async-start(), calls=%async_computation.17 | async-start | bytes 1769472 | tf_op jit(solution)/shard_map/all_gather | solution.py:295
  83.0 10.5 copy-start.61
  85.0 5.1 copy-start.128
  85.0 5.8 copy-start.117
  85.0 6.4 copy-start.126
  85.0 7.0 copy-start.125
  85.0 57.3 %all-to-all-start.1 = ((bf16[8,128,768]{1,2,0:T(8,128)(2,1)}), bf16[8,128,768]{1,2,0:T(8,128)(2,1)S(1)}, u32[]{:S(2)}, u32[]{:S(2)}) async-start(bf16[8,128,768]{1,2,0:T(8,128)(2,1)} %stack.18), calls=%async_computation.1 | async-start | bytes 3145728 | tf_op jit(solution)/shard_map/all_to_all | solution.py:11
  89.5 384.3 %all-gather.21.cloned.1.call-start = ((), (), s32[]{:S(2)}) async-start(), calls=%async_computation.16 | async-start | bytes 1769472 | tf_op jit(solution)/shard_map/all_gather | solution.py:295
  143.7 66.7 %all-to-all-start = ((bf16[8,128,768]{1,2,0:T(8,128)(2,1)}), bf16[8,128,768]{1,2,0:T(8,128)(2,1)}, u32[]{:S(2)}, u32[]{:S(2)}) async-start(bf16[8,128,768]{1,2,0:T(8,128)(2,1)} %stack.16), calls=%async_computation | async-start | bytes 3145728 | tf_op jit(solution)/shard_map/all_to_all | solution.py:11
  148.0 391.6 %reduce-scatter.31.cloned.1.call-start = ((), (), s32[]{:S(2)}) async-start(), calls=%async_computation.25 | async-start | bytes 1769472
  170.4 42.7 %copy-start.5 = (bf16[1024,768]{0,1:T(8,128)(2,1)}, bf16[1024,768]{0,1:T(8,128)(2,1)S(1)}, u32[]{:S(2)}) copy-start(bf16[1024,768]{0,1:T(8,128)(2,1)S(1)} %get-tuple-element.2086) | copy-start | bytes 4718596
  170.4 42.7 %copy-start.6 = (bf16[128,12,64]{0,2,1:T(8,128)(2,1)}, bf16[128,12,64]{0,2,1:T(8,128)(2,1)S(1)}, u32[]{:S(2)}) copy-start(bf16[128,12,64]{0,2,1:T(8,128)(2,1)S(1)} %get-tuple-element.2094) | copy-start | bytes 589828
  171.8 41.3 %copy-start.57 = (bf16[128,12,64]{0,2,1:T(8,128)(2,1)}, bf16[128,12,64]{0,2,1:T(8,128)(2,1)S(1)}, u32[]{:S(2)}) copy-start(bf16[128,12,64]{0,2,1:T(8,128)(2,1)S(1)} %fusion.137) | copy-start | bytes 589828
  270.8 55.6 %copy-start.4 = (bf16[1024,768]{0,1:T(8,128)(2,1)}, bf16[1024,768]{0,1:T(8,128)(2,1)S(1)}, u32[]{:S(2)}) copy-start(bf16[1024,768]{0,1:T(8,128)(2,1)S(1)} %get-tuple-element.2085) | copy-start | bytes 4718596
  270.8 46.9 %copy-start.28 = (f32[128,768]{1,0:T(8,128)S(1)}, f32[128,768]{1,0:T(8,128)}, u32[]{:S(2)}) copy-start(f32[128,768]{1,0:T(8,128)} %copy-done.27) | copy-start | bytes 1179652
  270.8 46.9 %copy-start.78 = (f32[768]{0:T(1024)S(1)}, f32[768]{0:T(1024)}, u32[]{:S(2)}) copy-start(f32[768]{0:T(1024)} %convert_element_type.274) | copy-start | bytes 9220
  270.8 46.8 %copy-start.84 = (f32[768]{0:T(1024)S(1)}, f32[768]{0:T(1024)}, u32[]{:S(2)}) copy-start(f32[768]{0:T(1024)} %convert_element_type.275) | copy-start | bytes 9220
  270.8 46.8 %copy-start.106 = (f32[3072]{0:T(1024)S(1)}, f32[3072]{0:T(1024)}, u32[]{:S(2)}) copy-start(f32[3072]{0:T(1024)} %convert_element_type.277) | copy-start | bytes 36868
  270.8 46.8 %copy-start.108 = (f32[128]{0:T(128)S(1)}, f32[128]{0:T(128)}, u32[]{:S(2)}) copy-start(f32[128]{0:T(128)} %copy-done.107) | copy-start | bytes 1540
  270.8 46.8 %copy-start.118 = (f32[128]{0:T(128)S(1)}, f32[128]{0:T(128)}, u32[]{:S(2)}) copy-start(f32[128]{0:T(128)} %fusion.145) | copy-start | bytes 1540
  272.4 53.9 %copy-start.63 = (bf16[128,12,64]{0,2,1:T(8,128)(2,1)}, bf16[128,12,64]{0,2,1:T(8,128)(2,1)S(1)}, u32[]{:S(2)}) copy-start(bf16[128,12,64]{0,2,1:T(8,128)(2,1)S(1)} %fusion.136) | copy-start | bytes 589828
  274.2 122.4 %copy-start.18 = (f32[128,768]{1,0:T(8,128)}, f32[128,768]{1,0:T(8,128)S(1)}, u32[]{:S(2)}) copy-start(f32[128,768]{1,0:T(8,128)S(1)} %get-tuple-element.1633) | copy-start | bytes 1179652
  274.2 52.1 %copy-start.100 = (f32[128]{0:T(128)}, f32[128]{0:T(128)S(1)}, u32[]{:S(2)}) copy-start(f32[128]{0:T(128)S(1)} %broadcast_multiply_fusion.2) | copy-start | bytes 1540
  274.4 51.9 %copy-start.135 = (f32[128]{0:T(128)}, f32[128]{0:T(128)S(1)}, u32[]{:S(2)}) copy-start(f32[128]{0:T(128)S(1)} %multiply_reduce_fusion.7) | copy-start | bytes 1540
  274.5 51.9 %copy-start.114 = (f32[128]{0:T(128)}, f32[128]{0:T(128)S(1)}, u32[]{:S(2)}) copy-start(f32[128]{0:T(128)S(1)} %fusion.143) | copy-start | bytes 1540
  317.7 8.7 copy-start.16
  326.4 55.9 %copy-start.45 = (bf16[2,1,128,768]{3,2,1,0:T(8,128)(2,1)S(1)}, bf16[2,1,128,768]{3,2,1,0:T(8,128)(2,1)}, u32[]{:S(2)}) copy-start(bf16[2,1,128,768]{3,2,1,0:T(8,128)(2,1)} %param.25) | copy-start | bytes 1179652
  382.3 5.8 copy-start.17
  382.3 7.5 copy-start.137
  382.3 7.5 copy-start.138
  469.6 137.7 %reduce-scatter.29.cloned.1.call-start = ((), (), s32[]{:S(2)}) async-start(), calls=%async_computation.24 | async-start | bytes 1769472
  473.7 201.3 %reduce-scatter.27.cloned.1.call-start = ((), (), s32[]{:S(2)}) async-start(), calls=%async_computation.23 | async-start | bytes 1769472
  515.7 226.9 %reduce-scatter.25.cloned.1.call-start = ((), (), s32[]{:S(2)}) async-start(), calls=%async_computation.22 | async-start | bytes 1769472
  518.7 328.5 %reduce-scatter.19.cloned.1.call-start = ((), (), s32[]{:S(2)}) async-start(), calls=%async_computation.19 | async-start | bytes 2433024 | tf_op jit(solution)/shard_map/reduce_scatter | solution.py:336
  522.0 221.7 %copy-start.10 = (bf16[2,1,128,768]{3,2,1,0:T(8,128)(2,1)S(1)}, bf16[2,1,128,768]{3,2,1,0:T(8,128)(2,1)}, u32[]{:S(2)}) copy-start(bf16[2,1,128,768]{3,2,1,0:T(8,128)(2,1)} %param.24) | copy-start | bytes 1179652
  522.1 221.7 %copy-start.76 = (f32[768]{0:T(1024)S(1)}, f32[768]{0:T(1024)}, u32[]{:S(2)}) copy-start(f32[768]{0:T(1024)} %copy-done.75) | copy-start | bytes 9220
  522.1 221.7 %copy-start.82 = (f32[768]{0:T(1024)S(1)}, f32[768]{0:T(1024)}, u32[]{:S(2)}) copy-start(f32[768]{0:T(1024)} %copy-done.81) | copy-start | bytes 9220
  522.1 221.7 %copy-start.89 = (f32[128]{0:T(128)S(1)}, f32[128]{0:T(128)}, u32[]{:S(2)}) copy-start(f32[128]{0:T(128)} %copy-done.88) | copy-start | bytes 1540
  522.1 221.7 %copy-start.104 = (f32[128]{0:T(128)S(1)}, f32[128]{0:T(128)}, u32[]{:S(2)}) copy-start(f32[128]{0:T(128)} %copy-done.103) | copy-start | bytes 1540
  522.1 449.9 %reduce-scatter.17.cloned.1.call-start = ((), (), s32[]{:S(2)}) async-start(), calls=%async_computation.18 | async-start | bytes 7299072 | tf_op jit(solution)/shard_map/reduce_scatter | solution.py:336
  523.2 221.9 %copy-start.69 = (bf16[128,12,64]{0,2,1:T(8,128)(2,1)}, bf16[128,12,64]{0,2,1:T(8,128)(2,1)S(1)}, u32[]{:S(2)}) copy-start(bf16[128,12,64]{0,2,1:T(8,128)(2,1)S(1)} %get-tuple-element.1579) | copy-start | bytes 589828
  524.0 221.0 %copy-start.73 = (bf16[128,12,64]{0,2,1:T(8,128)(2,1)}, bf16[128,12,64]{0,2,1:T(8,128)(2,1)S(1)}, u32[]{:S(2)}) copy-start(bf16[128,12,64]{0,2,1:T(8,128)(2,1)S(1)} %get-tuple-element.1581) | copy-start | bytes 589828
  608.4 136.7 %copy-start.67 = (bf16[128,768]{0,1:T(8,128)(2,1)}, bf16[128,768]{0,1:T(8,128)(2,1)S(1)}, u32[]{:S(2)}) copy-start(bf16[128,768]{0,1:T(8,128)(2,1)S(1)} %copy.186) | copy-start | bytes 589828
  749.3 364.0 %reduce-scatter.21.cloned.1.call-start = ((), (), s32[]{:S(2)}) async-start(), calls=%async_computation.20 | async-start | bytes 9732096 | tf_op jit(solution)/shard_map/reduce_scatter | solution.py:336
  757.2 497.6 %reduce-scatter.23.cloned.1.call-start = ((), (), s32[]{:S(2)}) async-start(), calls=%async_computation.21 | async-start | bytes 9732096 | tf_op jit(solution)/shard_map/reduce_scatter | solution.py:336
  765.0 6.5 copy-start.94
  785.1 46.9 %copy-start.49 = (f32[128,768]{1,0:T(8,128)S(1)}, f32[128,768]{1,0:T(8,128)}, u32[]{:S(2)}) copy-start(f32[128,768]{1,0:T(8,128)} %copy-done.48) | copy-start | bytes 1179652
  785.1 46.9 %copy-start.51 = (f32[128,768]{1,0:T(8,128)S(1)}, f32[128,768]{1,0:T(8,128)}, u32[]{:S(2)}) copy-start(f32[128,768]{1,0:T(8,128)} %copy-done.50) | copy-start | bytes 1179652
  785.1 46.9 %copy-start.122 = (f32[128]{0:T(128)S(1)}, f32[128]{0:T(128)}, u32[]{:S(2)}) copy-start(f32[128]{0:T(128)} %copy-done.121) | copy-start | bytes 1540
  785.1 46.9 %copy-start.124 = (f32[128]{0:T(128)S(1)}, f32[128]{0:T(128)}, u32[]{:S(2)}) copy-start(f32[128]{0:T(128)} %copy-done.123) | copy-start | bytes 1540
  (115 other events, 223.7 us)
Sparse Core Ops, SparseCore 0:
  10.9 62.8 all-gather.8
  77.4 63.7 all-gather.18
  144.2 63.0 all-gather.12
  209.8 43.0 all-gather.10
  255.7 61.8 all-gather.14
  320.4 61.8 all-gather.16
  385.0 42.5 all-gather.22
  429.8 42.5 all-gather.20
  475.8 63.8 reduce-scatter.30
  543.0 64.2 reduce-scatter.28
  610.7 64.2 reduce-scatter.26
  678.3 64.2 reduce-scatter.24
  748.5 98.7 reduce-scatter.18
  853.4 118.5 reduce-scatter.16
  978.3 135.0 reduce-scatter.20
  1119.7 135.1 reduce-scatter.22
